TPU v7x, 32 devices: a whole 2x2x4 slice. The times are simulated.
32 devices in a mesh: space: 4 (over z), dp: 8 (over y, x, core).
Axes of the slice: x: 2, y: 2, z: 4, core: 2. Of those that a mesh axis runs over, the one named last changes fastest.
Arguments:
- features: bfloat16 [8, 12, 128, 320], P('dp', 'space'), may hold values from -6 to 6
- cotangent: bfloat16 [8, 12, 128, 320], P('dp', 'space'), may hold values from -6 to 6
- norm_gain: float32 [320], replicated, may hold values from 0.1 to 1.9
- norm_bias: float32 [320], replicated, may hold values from -0.5 to 0.5
- weight: bfloat16 [2880, 320], P('dp'), may hold values from -0.109375 to 0.109375
- moment_one: float32 [2880, 320], P('dp'), may hold values from -332.55374 to 332.55374
- moment_two: float32 [2880, 320], P('dp'), may hold values from 768 to 6144
- heights: int32 [8], P('dp'), may hold values from 6 to 12, as said below
- widths: int32 [8], P('dp'), may hold values from 64 to 128, as said below
Outputs:
- block_out: bfloat16 [8, 12, 128, 320], P('dp', 'space')
- input_grad: bfloat16 [8, 12, 128, 320], P('dp', 'space')
- weight_grad: float32 [2880, 320], P('dp')
- adam_update: float32 [2880, 320], P('dp')
Inputs may be any that keep to these rules, and one draw needn't show every extreme that they name: Image i occupies canvas rows 0 to heights[i] - 1; some image has all 12 rows. Image i occupies canvas columns 0 to widths[i] - 1; some image has all 128 columns.
All inputs are finite; a program needn't handle non-finite values.
Results may differ from a plain program's by a relative error of at most 0.017.
Values may be sent and summed in bfloat16 or wider, within the bound.
No kernel may reach another device: no remote copies, remote signals or barrier semaphores. Data moves between devices by JAX's collectives and lax.ppermute only.
A program may use at most 64 MiB of HBM per device.

v0:
```python
import jax
import jax.numpy as jnp
from jax import lax
from jax.sharding import PartitionSpec as P

GROUPS = 32


def with_halo(cells, sides, width):
    for axis, dim in sides:
        count = lax.axis_size(axis)
        ends = count - 1
        head = lax.slice_in_dim(cells, 0, width, axis=dim)
        tail = lax.slice_in_dim(cells, cells.shape[dim] - width, cells.shape[dim], axis=dim)
        cells = jnp.concatenate(
            [
                lax.ppermute(tail, axis, [(i, (i + 1) % count) for i in range(ends)]),
                cells,
                lax.ppermute(head, axis, [((i + 1) % count, i) for i in range(ends)]),
            ],
            axis=dim,
        )
    return cells


def group_sum(values, groups):
    height_dev, width_dev, channels = values.shape
    return values.reshape(height_dev, width_dev, groups, channels // groups).sum(axis=(0, 1, 3))


def spread_groups(statistic, channels):
    return jnp.repeat(statistic, channels // statistic.shape[0])


def pad_columns(padded_rows):
    return jnp.pad(padded_rows, ((0, 0), (1, 1), (0, 0)))


def local(
    features, cotangent, norm_gain, norm_bias, weight, moment_one, moment_two, heights, widths
):
    latent = features[0]
    height_dev, width_dev, channels = latent.shape
    row_ids = lax.axis_index("space") * height_dev + jnp.arange(height_dev, dtype=jnp.int32)
    inside = (
        (row_ids < heights[0])[:, None]
        & (jnp.arange(width_dev, dtype=jnp.int32) < widths[0])[None, :]
    ).astype(jnp.float32)[..., None]
    cell_count = (heights[0] * widths[0] * (channels // GROUPS)).astype(jnp.float32)
    gathered = lax.all_gather(weight, "dp", axis=0, tiled=True)
    tap_weights = gathered.reshape(9, channels, channels)
    values = latent.astype(jnp.float32) * inside
    group_total, squares = lax.psum(
        (group_sum(values, GROUPS), group_sum(values * values, GROUPS)), "space"
    )
    center = group_total / cell_count
    spread = squares / cell_count - center * center
    inverse = lax.rsqrt(spread + 1e-05)
    normed = (values - spread_groups(center, channels)) * spread_groups(inverse, channels) * inside
    before = normed * norm_gain + norm_bias
    activated = (jax.nn.silu(before) * inside).astype(jnp.bfloat16)
    act_pad = pad_columns(with_halo(activated, (("space", 0),), 1))
    output = jnp.zeros((height_dev * width_dev, channels), jnp.float32)
    for row_off in range(3):
        for col_off in range(3):
            window = act_pad[row_off : row_off + height_dev, col_off : col_off + width_dev].reshape(
                -1, channels
            )
            output = output + jnp.dot(
                window, tap_weights[row_off * 3 + col_off], preferred_element_type=jnp.float32
            )
    block_out = (output.reshape(height_dev, width_dev, channels) * inside).astype(jnp.bfloat16)
    masked = cotangent[0] * inside.astype(jnp.bfloat16)
    cot_pad = pad_columns(with_halo(masked, (("space", 0),), 1))
    flat_cot = masked.reshape(-1, channels)
    upstream = jnp.zeros((height_dev * width_dev, channels), jnp.float32)
    tap_grads = []
    for row_off in range(3):
        for col_off in range(3):
            tap_index = row_off * 3 + col_off
            window = act_pad[row_off : row_off + height_dev, col_off : col_off + width_dev].reshape(
                -1, channels
            )
            tap_grads.append(
                lax.dot_general(
                    window, flat_cot, (((0,), (0,)), ((), ())), preferred_element_type=jnp.float32
                )
            )
            cot_window = cot_pad[
                2 - row_off : 2 - row_off + height_dev, 2 - col_off : 2 - col_off + width_dev
            ].reshape(-1, channels)
            upstream = upstream + lax.dot_general(
                cot_window,
                tap_weights[tap_index],
                (((1,), (1,)), ((), ())),
                preferred_element_type=jnp.float32,
            )
    weight_terms = jnp.stack(tap_grads).reshape(9 * channels, channels)
    gate_sig = jax.nn.sigmoid(before)
    silu_slope = gate_sig * (1.0 + before * (1.0 - gate_sig))
    scaled = upstream.reshape(height_dev, width_dev, channels) * silu_slope * inside * norm_gain
    local_first = group_sum(scaled, GROUPS)
    local_second = group_sum(scaled * normed, GROUPS)
    grad_piece = lax.psum_scatter(weight_terms, "dp", scatter_dimension=0, tiled=True)
    sum_first, sum_second = lax.psum((local_first, local_second), "space")
    grad_piece = lax.psum(grad_piece.astype(jnp.bfloat16), "space").astype(jnp.float32)
    first = sum_first / cell_count
    second = sum_second / cell_count
    input_grad = (
        spread_groups(inverse, channels)
        * (scaled - spread_groups(first, channels) - normed * spread_groups(second, channels))
        * inside
    ).astype(jnp.bfloat16)
    first_new = 0.9 * moment_one + 0.1 * grad_piece
    second_new = 0.999 * moment_two + 0.001 * grad_piece * grad_piece
    adam_update = first_new / (1.0 - 0.9**10) / (jnp.sqrt(second_new / (1.0 - 0.999**10)) + 1e-08)
    return (block_out[None], input_grad[None], grad_piece, adam_update)


def solution(mesh):
    placed = (
        P("dp", "space", None, None),
        P("dp", "space", None, None),
        P(),
        P(),
        P("dp", None),
        P("dp", None),
        P("dp", None),
        P("dp"),
        P("dp"),
    )
    return jax.shard_map(
        local,
        mesh=mesh,
        in_specs=placed,
        out_specs=(
            P("dp", "space", None, None),
            P("dp", "space", None, None),
            P("dp", None),
            P("dp", None),
        ),
        check_vma=False,
    )
```

profile of v0, /device:TPU:0, one launch (start us, length us, event | category | flops | bytes accessed | tf_op | source)
XLA Modules:
  0.0 207.1 jit_solution(10719719046943289507)
XLA Ops:
  9.4 1.1 multiply_reduce_fusion.1
  11.0 13.5 %all-reduce.4 = (f32[32]{0:T(128)S(1)}, f32[32]{0:T(128)S(1)}) all-reduce(f32[32]{0:T(128)S(1)} %reduce_sum.51, f32[32]{0:T(128)S(1)} %reduce_sum.54), channel_id=1, replica_groups=mesh['space'=4,'dp'=8] {'space'}, use_global_device_ids=true, to_apply=%region_2.0 | all-reduce | flops 64 | bytes 512 | tf_op jit(solution)/shard_map/psum | solution.py:53
  24.9 1.3 multiply_convert_fusion.4
  26.2 1.3 collective-permute-start
  27.5 1.3 collective-permute-start.1
  28.8 1.0 bitcast_multiply_fusion.2
  29.8 1.2 dynamic-slice
  31.7 2.1 %collective-permute-done.1 = bf16[1,128,320]{1,2,0:T(8,128)(2,1)S(1)} collective-permute-done((bf16[1,128,320]{1,2,0:T(8,128)(2,1)S(1)}, bf16[1,128,320]{1,2,0:T(8,128)(2,1)S(1)}, u32[]{:S(2)}, u32[]{:S(2)}) %collective-permute-start.1) | collective-permute-done | bytes 81952 | tf_op jit(solution)/shard_map/ppermute | solution.py:19
  34.3 1.1 fusion.9
  35.4 1.1 fusion.2
  36.5 1.2 fusion.8
  37.6 1.1 fusion.7
  38.7 1.3 fusion.6
  40.0 1.2 fusion.5
  41.2 1.1 fusion.4
  42.3 1.1 fusion.1
  43.4 1.1 fusion.3
  44.5 5.6 %copy.68 = f32[2880,320]{0,1:T(8,128)} copy(f32[2880,320]{1,0:T(8,128)} %bitcast.48) | data formatting | bytes 7372800 | tf_op jit(solution)/shard_map/reshape | solution.py:98
  50.2 80.3 %all-reduce.9 = bf16[2880,320]{0,1:T(8,128)(2,1)S(1)} all-reduce(f32[2880,320]{0,1:T(8,128)} %copy.68), channel_id=2, replica_groups=mesh['space'=4,'dp'=8] {'dp'}, use_global_device_ids=true, to_apply=%region_12.13.clone | all-reduce | flops 921600 | bytes 5529600
  130.5 0.8 dynamic-slice_convert_fusion
  132.6 2.7 %collective-permute-start.2 = (bf16[1,128,320]{1,2,0:T(8,128)(2,1)}, bf16[1,128,320]{1,2,0:T(8,128)(2,1)S(1)}, u32[]{:S(2)}, u32[]{:S(2)}) collective-permute-start(bf16[1,128,320]{1,2,0:T(8,128)(2,1)} %get-tuple-element.30), channel_id=1, source_target_pairs={{0,8},{8,16},{16,24},{1,9},{9,17},{17,25},{2,10},{10,18},{18,26},{... | collective-permute-start | bytes 245768 | tf_op jit(solution)/shard_map/ppermute | solution.py:17
  135.2 1.5 collective-permute-start.3
  136.9 1.2 copy.60
  138.1 1.0 copy.49
  139.3 1.1 fusion.84
  140.4 1.2 copy.43
  141.6 0.9 copy.45
  142.5 0.9 copy.46
  143.5 0.9 copy.47
  144.4 0.9 copy.51
  145.2 0.9 copy.50
  147.4 0.9 copy.56
  149.0 1.9 copy.57
  150.9 0.9 copy.58
  151.8 0.9 copy.59
  152.7 0.9 copy.61
  153.6 0.9 copy.62
  154.5 0.9 copy.63
  155.3 0.9 copy.64
  156.3 8.3 %all-reduce.8.cloned.1.call-done = bf16[360,320]{0,1:T(8,128)(2,1)} async-done(((bf16[360,320]{0,1:T(8,128)(2,1)}), bf16[360,320]{0,1:T(8,128)(2,1)}) %all-reduce.8.cloned.1.call-update) | async-done | bytes 230416 | tf_op jit(solution)/shard_map/psum | solution.py:106
  164.5 2.5 %fusion.17 = (f32[360,320]{0,1:T(8,128)}, f32[360,320]{0,1:T(8,128)}) fusion(f32[360,320]{0,1:T(8,128)} %param.15, f32[360,320]{0,1:T(8,128)} %param.14, bf16[360,320]{0,1:T(8,128)(2,1)} %all-reduce.8.cloned.1.call-done), kind=kLoop, calls=%fused_computation.47 | loop fusion | flops 1382400 | bytes 2073600 | tf_op jit(solution)/shard_map/div | solution.py:116
  167.0 3.9 %copy.44 = bf16[8,360,320]{1,0,2:T(8,128)(2,1)} copy(bf16[8,360,320]{1,2,0:T(8,128)(2,1)} %all-gather.3.cloned.1.call-done) | data formatting | bytes 3686400 | tf_op jit(solution)/shard_map/all_gather | solution.py:50
  170.9 3.4 %reshape.284 = bf16[2880,320]{0,1:T(8,128)(2,1)S(1)} reshape(bf16[8,360,320]{1,0,2:T(8,128)(2,1)} %copy.44) | data formatting | bytes 3686400
  174.7 1.3 fusion.50
  179.6 1.4 fusion.63
  181.0 1.5 convolution_add_fusion.8
  186.7 10.8 %all-reduce.3 = (f32[32]{0:T(128)S(1)}, f32[32]{0:T(128)S(1)}) all-reduce(f32[32]{0:T(128)S(1)} %reduce_sum.75, f32[32]{0:T(128)S(1)} %reduce_sum.72), channel_id=1, replica_groups=mesh['space'=4,'dp'=8] {'space'}, use_global_device_ids=true, to_apply=%region_11.12 | all-reduce | flops 64 | bytes 512 | tf_op jit(solution)/shard_map/psum | solution.py:105
  198.4 1.3 multiply_convert_fusion.1
  (102 shorter events, 13.6 us)
Async XLA Ops:
  8.0 156.5 %all-reduce.8.cloned.1.call-start = ((), (), s32[]{:S(2)}) async-start(), calls=%async_computation | async-start | bytes 491520 | tf_op jit(solution)/shard_map/psum | solution.py:106
  26.2 5.5 %collective-permute-start = (bf16[1,128,320]{1,2,0:T(8,128)(2,1)S(1)}, bf16[1,128,320]{1,2,0:T(8,128)(2,1)S(1)}, u32[]{:S(2)}, u32[]{:S(2)}) collective-permute-start(bf16[1,128,320]{1,2,0:T(8,128)(2,1)S(1)} %get-tuple-element.34), channel_id=1, source_target_pairs={{0,8},{8,16},{16,24},{1,9},{9,17},{17,25},{2,10},{10,18},{18,26},{... | collective-permute-start | bytes 245768 | tf_op jit(solution)/shard_map/ppermute | solution.py:17
  27.5 6.3 %collective-permute-start.1 = (bf16[1,128,320]{1,2,0:T(8,128)(2,1)S(1)}, bf16[1,128,320]{1,2,0:T(8,128)(2,1)S(1)}, u32[]{:S(2)}, u32[]{:S(2)}) collective-permute-start(bf16[1,128,320]{1,2,0:T(8,128)(2,1)S(1)} %get-tuple-element.35), channel_id=1, source_target_pairs={{8,0},{16,8},{24,16},{9,1},{17,9},{25,17},{10,2},{18,10},{26,18},{... | collective-permute-start | bytes 245768 | tf_op jit(solution)/shard_map/ppermute | solution.py:19
  31.7 6.0 %copy-start.12 = (bf16[1,128,320]{1,2,0:T(8,128)(2,1)}, bf16[1,128,320]{1,2,0:T(8,128)(2,1)S(1)}, u32[]{:S(2)}) copy-start(bf16[1,128,320]{1,2,0:T(8,128)(2,1)S(1)} %collective-permute-done) | copy-start | bytes 245764
  33.8 8.5 %copy-start.14 = (bf16[1,128,320]{1,2,0:T(8,128)(2,1)}, bf16[1,128,320]{1,2,0:T(8,128)(2,1)S(1)}, u32[]{:S(2)}) copy-start(bf16[1,128,320]{1,2,0:T(8,128)(2,1)S(1)} %collective-permute-done.1) | copy-start | bytes 245764
  34.2 4.5 %copy-start = (bf16[1,3,128,320]{2,3,1,0:T(8,128)(2,1)S(1)}, bf16[1,3,128,320]{2,3,1,0:T(8,128)(2,1)}, u32[]{:S(2)}) copy-start(bf16[1,3,128,320]{2,3,1,0:T(8,128)(2,1)} %param.9) | copy-start | bytes 737284
  34.2 4.5 %copy-start.10 = (bf16[1,3,128,320]{2,3,1,0:T(8,128)(2,1)S(1)}, bf16[1,3,128,320]{2,3,1,0:T(8,128)(2,1)}, u32[]{:S(2)}) copy-start(bf16[1,3,128,320]{2,3,1,0:T(8,128)(2,1)} %param.10) | copy-start | bytes 737284
  34.2 4.5 %copy-start.19 = (f32[320]{0:T(512)S(1)}, f32[320]{0:T(512)}, u32[]{:S(2)}) copy-start(f32[320]{0:T(512)} %param.12) | copy-start | bytes 3844
  34.2 4.5 %copy-start.20 = (f32[320]{0:T(512)S(1)}, f32[320]{0:T(512)}, u32[]{:S(2)}) copy-start(f32[320]{0:T(512)} %param.11) | copy-start | bytes 3844
  131.3 35.7 %all-gather.3.cloned.1.call-start = ((), (), s32[]{:S(2)}) async-start(), calls=%async_computation.1 | async-start | bytes 2211840 | tf_op jit(solution)/shard_map/all_gather | solution.py:50
  132.6 14.1 %collective-permute-start.2 = (bf16[1,128,320]{1,2,0:T(8,128)(2,1)}, bf16[1,128,320]{1,2,0:T(8,128)(2,1)S(1)}, u32[]{:S(2)}, u32[]{:S(2)}) collective-permute-start(bf16[1,128,320]{1,2,0:T(8,128)(2,1)} %get-tuple-element.30), channel_id=1, source_target_pairs={{0,8},{8,16},{16,24},{1,9},{9,17},{17,25},{2,10},{10,18},{18,26},{... | collective-permute-start | bytes 245768 | tf_op jit(solution)/shard_map/ppermute | solution.py:17
  135.2 11.4 %collective-permute-start.3 = (bf16[1,128,320]{1,2,0:T(8,128)(2,1)}, bf16[1,128,320]{1,2,0:T(8,128)(2,1)S(1)}, u32[]{:S(2)}, u32[]{:S(2)}) collective-permute-start(bf16[1,128,320]{1,2,0:T(8,128)(2,1)} %get-tuple-element.31), channel_id=1, source_target_pairs={{8,0},{16,8},{24,16},{9,1},{17,9},{25,17},{10,2},{18,10},{26,18},{... | collective-permute-start | bytes 245768 | tf_op jit(solution)/shard_map/ppermute | solution.py:19
  139.3 2.3 %copy-start.13 = (bf16[1,128,320]{1,2,0:T(8,128)(2,1)S(1)}, bf16[1,128,320]{1,2,0:T(8,128)(2,1)}, u32[]{:S(2)}) copy-start(bf16[1,128,320]{1,2,0:T(8,128)(2,1)} %copy-done.12) | copy-start | bytes 245764
  139.3 2.3 %copy-start.15 = (bf16[1,128,320]{1,2,0:T(8,128)(2,1)S(1)}, bf16[1,128,320]{1,2,0:T(8,128)(2,1)}, u32[]{:S(2)}) copy-start(bf16[1,128,320]{1,2,0:T(8,128)(2,1)} %copy-done.14) | copy-start | bytes 245764
  140.4 2.2 %copy-start.11 = (bf16[3,128,320]{1,2,0:T(8,128)(2,1)S(1)}, bf16[3,128,320]{1,2,0:T(8,128)(2,1)}, u32[]{:S(2)}) copy-start(bf16[3,128,320]{1,2,0:T(8,128)(2,1)} %get-tuple-element.26) | copy-start | bytes 737284
  174.3 1.7 copy-start.7
  174.3 2.1 %copy-start.3 = (bf16[3,128,320]{2,1,0:T(8,128)(2,1)S(1)}, bf16[3,128,320]{2,1,0:T(8,128)(2,1)}, u32[]{:S(2)}) copy-start(bf16[3,128,320]{2,1,0:T(8,128)(2,1)} %copy.45) | copy-start | bytes 737284
  174.7 2.2 %copy-start.2 = (bf16[3,128,320]{2,1,0:T(8,128)(2,1)S(1)}, bf16[3,128,320]{2,1,0:T(8,128)(2,1)}, u32[]{:S(2)}) copy-start(bf16[3,128,320]{2,1,0:T(8,128)(2,1)} %copy.46) | copy-start | bytes 737284
  176.0 1.1 copy-start.1
  176.8 1.1 copy-start.16
  179.6 2.9 %copy-start.9 = (bf16[3,128,320]{2,1,0:T(8,128)(2,1)S(1)}, bf16[3,128,320]{2,1,0:T(8,128)(2,1)}, u32[]{:S(2)}) copy-start(bf16[3,128,320]{2,1,0:T(8,128)(2,1)} %copy.58) | copy-start | bytes 737284
  179.6 3.3 %copy-start.8 = (bf16[3,128,320]{2,1,0:T(8,128)(2,1)S(1)}, bf16[3,128,320]{2,1,0:T(8,128)(2,1)}, u32[]{:S(2)}) copy-start(bf16[3,128,320]{2,1,0:T(8,128)(2,1)} %copy.59) | copy-start | bytes 737284
  182.9 1.0 copy-start.6
  183.5 1.0 copy-start.4
  183.9 1.0 copy-start.5
  184.4 1.1 copy-start.17
  184.4 1.1 copy-start.18
Sparse Core Ops, SparseCore 0:
  131.4 33.0 all-reduce.7
Sparse Core Ops, SparseCore 1:
  133.7 24.6 all-gather.2
where the time goes:
time: 208 us; the launch traced here: 207 us
  blocking collectives  105 us (50%)
  local copies, waits for them, and re-layouts  36.4 us (18%)
  matrix products  20.9 us (10%)
  between operations  18 us (9%)
  waiting for transfers between devices  10.9 us (5%)
  other arithmetic  9.44 us (5%)
  starting transfers between devices  6.8 us (3%)
    unnamed x1, blocking collectives  80.3 us
    psum x1, blocking collectives, local(): lax.psum((group_sum(values, GROUPS), group_sum(values * values, GROUPS)),...  13.5 us
    psum x1, blocking collectives, local(): sum_first, sum_second = lax.psum((local_first, local_second), 'space')  10.8 us
    dot_general x9, matrix products, local(): lax.dot_general(window, flat_cot, (((0,), (0,)), ((), ())), preferred_ele...  10.3 us
    slice x9, local copies, waits for them, and re-layouts, local(): cot_pad[2 - row_off:2 - row_off + height_dev, 2 - col_off:2 - col_off + w...  8.48 us
    psum x1, waiting for transfers between devices, local(): lax.psum(grad_piece.astype(jnp.bfloat16), 'space').astype(jnp.float32)  8.25 us
    slice x9, local copies, waits for them, and re-layouts, local(): act_pad[row_off:row_off + height_dev, col_off:col_off + width_dev]  7.27 us
    unnamed x45, local copies, waits for them, and re-layouts  6.36 us
  transfers between devices with their start and end apart: 6, of which 2 were waited for; matrix products, arithmetic and copies ran while one was open for 12% of the time, Pallas kernels for 0%

commit v1 on v0

--- a/solution.py
+++ b/solution.py
@@ -103,7 +103,9 @@
     local_second = group_sum(scaled * normed, GROUPS)
     grad_piece = lax.psum_scatter(weight_terms, "dp", scatter_dimension=0, tiled=True)
     sum_first, sum_second = lax.psum((local_first, local_second), "space")
-    grad_piece = lax.psum(grad_piece.astype(jnp.bfloat16), "space").astype(jnp.float32)
+    grad_piece = jnp.sum(lax.all_gather(grad_piece.astype(jnp.bfloat16), "space"), axis=0).astype(
+        jnp.float32
+    )
     first = sum_first / cell_count
     second = sum_second / cell_count
     input_grad = (

time: 208 us -> 146 us (0.70)
  blocking collectives: 105 us -> 46.5 us
  matrix products: 20.9 us -> 15.4 us
  local copies, waits for them, and re-layouts: 36.4 us -> 39.1 us
  waiting for transfers between devices: 10.9 us -> 8.52 us
  starting transfers between devices: 6.8 us -> 9.12 us
    unnamed x1 -> x0, blocking collectives: 80.3 us -> none
    all_gather x0 -> x1, blocking collectives: none -> 21.9 us  [local(): lax.all_gather(grad_piece.astype(jnp.bfloat16), 'space')]
    psum x1 -> x0, waiting for transfers between devices: 8.25 us -> none  [local(): lax.psum(grad_piece.astype(jnp.bfloat16), 'space').astype(jnp.float32)]
    unnamed x2 -> x3, waiting for transfers between devices: 0.54 us -> 8.5 us
    dot_general x9, matrix products: 10.3 us -> 3.19 us  [local(): lax.dot_general(window, flat_cot, (((0,), (0,)), ((), ())), preferred_ele...]
    reshape x1 -> x0, local copies, waits for them, and re-layouts: 5.63 us -> none  [local(): weight_terms = jnp.stack(tap_grads).reshape(9 * channels, channels)]
    unnamed x45 -> x58, local copies, waits for them, and re-layouts: 6.36 us -> 11.7 us
    ppermute x2, starting transfers between devices: 3.96 us -> 6.47 us  [with_halo(): lax.ppermute(tail, axis, [(i, (i + 1) % count) for i in range(ends)])]
  transfers between devices with their start and end apart: 6 -> 6, of which waited for: 2 -> 1; matrix products, arithmetic and copies ran while one was open for 12% -> 37% of each run, Pallas kernels for 0% -> 0%
where the time goes in v1:
time: 146 us; the launch traced here: 145 us
  blocking collectives  46.5 us (32%)
  local copies, waits for them, and re-layouts  39.1 us (27%)
  between operations  16.1 us (11%)
  matrix products  15.4 us (11%)
  other arithmetic  10.6 us (7%)
  starting transfers between devices  9.12 us (6%)
  waiting for transfers between devices  8.52 us (6%)
    all_gather x1, blocking collectives, local(): lax.all_gather(grad_piece.astype(jnp.bfloat16), 'space')  21.9 us
    psum x1, blocking collectives, local(): lax.psum((group_sum(values, GROUPS), group_sum(values * values, GROUPS)),...  13.5 us
    unnamed x58, local copies, waits for them, and re-layouts  11.7 us
    psum x1, blocking collectives, local(): sum_first, sum_second = lax.psum((local_first, local_second), 'space')  11.1 us
    slice x9, local copies, waits for them, and re-layouts, local(): act_pad[row_off:row_off + height_dev, col_off:col_off + width_dev]  8.86 us
    unnamed x3, waiting for transfers between devices  8.5 us
    slice x9, local copies, waits for them, and re-layouts, local(): cot_pad[2 - row_off:2 - row_off + height_dev, 2 - col_off:2 - col_off + w...  7.56 us
    dot_general x9, matrix products, local(): lax.dot_general(cot_window, tap_weights[tap_index], (((1,), (1,)), ((), (...  7.1 us
  transfers between devices with their start and end apart: 6, of which 1 were waited for; matrix products, arithmetic and copies ran while one was open for 37% of the time, Pallas kernels for 0%

profile of v1, /device:TPU:0, one launch (start us, length us, event | category | flops | bytes accessed | tf_op | source)
XLA Modules:
  0.0 145.4 jit_solution(11671311081981444725)
XLA Ops:
  8.7 1.1 multiply_reduce_fusion.1
  10.3 13.5 %all-reduce.4 = (f32[32]{0:T(128)S(1)}, f32[32]{0:T(128)S(1)}) all-reduce(f32[32]{0:T(128)S(1)} %reduce_sum.62, f32[32]{0:T(128)S(1)} %reduce_sum.81), channel_id=1, replica_groups=mesh['space'=4,'dp'=8] {'space'}, use_global_device_ids=true, to_apply=%region_2.0 | all-reduce | flops 64 | bytes 512 | tf_op jit(solution)/shard_map/psum | solution.py:53
  24.2 1.3 multiply_convert_fusion.4
  25.5 1.3 collective-permute-start
  26.8 1.3 collective-permute-start.1
  28.2 1.0 bitcast_multiply_fusion.2
  29.2 0.7 fusion.85
  29.9 5.2 %collective-permute-start.2 = (bf16[1,128,320]{1,2,0:T(8,128)(2,1)}, bf16[1,128,320]{1,2,0:T(8,128)(2,1)}, u32[]{:S(2)}, u32[]{:S(2)}) collective-permute-start(bf16[1,128,320]{1,2,0:T(8,128)(2,1)} %get-tuple-element.32), channel_id=1, source_target_pairs={{0,8},{8,16},{16,24},{1,9},{9,17},{17,25},{2,10},{10,18},{18,26},{... | collective-permute-start | bytes 245768 | tf_op jit(solution)/shard_map/ppermute | solution.py:17
  35.1 1.3 collective-permute-start.3
  36.6 0.8 bitcast_multiply_fusion.1
  37.9 2.1 %copy.69 = f32[360,320]{1,0:T(8,128)} copy(f32[360,320]{0,1:T(8,128)} %param.15) | data formatting | bytes 921600 | tf_op args[6]
  40.0 1.0 copy.47
  42.0 1.2 fusion.84
  43.2 1.2 copy.41
  47.9 2.0 %copy-done = f32[9,320,320]{2,1,0:T(8,128)} copy-done((f32[9,320,320]{2,1,0:T(8,128)}, f32[9,320,320]{2,1,0:T(8,128)S(1)}, u32[]{:S(2)}) %copy-start) | copy-done | bytes 3686424
  49.9 0.9 copy.43
  50.7 1.8 %copy.44 = bf16[3,128,320]{2,1,0:T(8,128)(2,1)} copy(bf16[3,128,320]{1,2,0:T(8,128)(2,1)} %get-tuple-element.28) | data formatting | bytes 491520 | tf_op jit(solution)/shard_map/slice | solution.py:66
  52.6 0.9 copy.45
  53.5 0.9 copy.49
  54.4 0.9 copy.48
  55.5 0.9 copy.51
  56.4 1.3 select_maximum_fusion
  58.1 0.9 copy.54
  59.0 1.0 pad_maximum_fusion
  60.0 0.9 copy.55
  60.9 0.9 copy.56
  61.8 0.9 copy.57
  62.7 0.9 copy.59
  63.6 0.9 copy.60
  64.5 0.9 copy.61
  65.4 0.9 copy.62
  66.3 4.2 %copy.42 = bf16[8,360,320]{1,0,2:T(8,128)(2,1)} copy(bf16[8,360,320]{1,2,0:T(8,128)(2,1)} %all-gather.5.cloned.1.call-done) | data formatting | bytes 3686400 | tf_op jit(solution)/shard_map/all_gather | solution.py:50
  70.6 3.5 %reshape.285 = bf16[2880,320]{0,1:T(8,128)(2,1)S(1)} reshape(bf16[8,360,320]{1,0,2:T(8,128)(2,1)} %copy.42) | data formatting | bytes 3686400
  74.4 1.3 fusion.50
  78.6 1.1 convolution_add_fusion.9
  79.7 1.3 copy.52
  80.9 1.0 copy.53
  82.0 1.5 %fusion.63 = f32[384,320]{0,1:T(8,128)S(1)} fusion(bf16[384,320]{1,0:T(8,128)(2,1)} %bitcast.155, bf16[2880,320]{0,1:T(8,128)(2,1)S(1)} %reshape.285), kind=kOutput, calls=%fused_computation.113 | convolution fusion | flops 78643200 | bytes 983040 | tf_op jit(solution)/shard_map/dot_general | solution.py:92
  83.4 1.5 %convolution_add_fusion.8 = f32[384,320]{0,1:T(8,128)S(1)} fusion(f32[384,320]{0,1:T(8,128)S(1)} %fusion.63, bf16[384,320]{1,0:T(8,128)(2,1)} %bitcast.159, bf16[2880,320]{0,1:T(8,128)(2,1)S(1)} %reshape.285), kind=kOutput, calls=%fused_computation.31 | convolution fusion | flops 78766080 | bytes 1474560 | tf_op jit(solution)/shard_map/dot_general | solution.py:92
  88.0 1.3 fusion.82
  89.8 11.1 %all-reduce.3 = (f32[32]{0:T(128)S(1)}, f32[32]{0:T(128)S(1)}) all-reduce(f32[32]{0:T(128)S(1)} %reduce_sum.87, f32[32]{0:T(128)S(1)} %reduce_sum.84), channel_id=1, replica_groups=mesh['space'=4,'dp'=8] {'space'}, use_global_device_ids=true, to_apply=%region_11.12 | all-reduce | flops 64 | bytes 512 | tf_op jit(solution)/shard_map/psum | solution.py:105
  101.3 1.3 copy.63
  102.8 1.3 multiply_convert_fusion.1
  104.1 8.5 %reduce-scatter.4.cloned.1.call-done = f32[360,320]{1,0:T(8,128)} async-done(((f32[2880,320]{1,0:T(8,128)}), f32[360,320]{1,0:T(8,128)}) %reduce-scatter.4.cloned.1.call-update) | async-done | bytes 460816
  112.6 1.1 convert_bitcast_fusion
  113.9 21.9 %all-gather.2 = bf16[4,360,320]{1,2,0:T(8,128)(2,1)S(1)} all-gather(bf16[1,360,320]{1,2,0:T(8,128)(2,1)S(1)} %copy.66), channel_id=2, replica_groups=mesh['space'=4,'dp'=8] {'space'}, dimensions={0}, use_global_device_ids=true | all-gather | bytes 1152000 | tf_op jit(solution)/shard_map/all_gather | solution.py:106
  136.3 0.9 copy.70
  137.6 1.0 copy.71
  (115 shorter events, 14.8 us)
Async XLA Ops:
  7.2 30.3 %copy-start.1 = (bf16[1,3,128,320]{2,3,1,0:T(8,128)(2,1)S(1)}, bf16[1,3,128,320]{2,3,1,0:T(8,128)(2,1)}, u32[]{:S(2)}) copy-start(bf16[1,3,128,320]{2,3,1,0:T(8,128)(2,1)} %param.9) | copy-start | bytes 737284
  7.2 29.2 %copy-start.15 = (bf16[1,3,128,320]{2,3,1,0:T(8,128)(2,1)S(1)}, bf16[1,3,128,320]{2,3,1,0:T(8,128)(2,1)}, u32[]{:S(2)}) copy-start(bf16[1,3,128,320]{2,3,1,0:T(8,128)(2,1)} %param.10) | copy-start | bytes 737284
  7.2 59.1 %all-gather.5.cloned.1.call-start = ((), (), s32[]{:S(2)}) async-start(), calls=%async_computation.1 | async-start | bytes 2211840 | tf_op jit(solution)/shard_map/all_gather | solution.py:50
  24.2 13.5 %copy-start.19 = (f32[360,320]{0,1:T(8,128)S(1)}, f32[360,320]{0,1:T(8,128)}, u32[]{:S(2)}) copy-start(f32[360,320]{0,1:T(8,128)} %param.14) | copy-start | bytes 1382404
  25.5 15.5 %collective-permute-start = (bf16[1,128,320]{1,2,0:T(8,128)(2,1)S(1)}, bf16[1,128,320]{1,2,0:T(8,128)(2,1)S(1)}, u32[]{:S(2)}, u32[]{:S(2)}) collective-permute-start(bf16[1,128,320]{1,2,0:T(8,128)(2,1)S(1)} %get-tuple-element.36), channel_id=1, source_target_pairs={{0,8},{8,16},{16,24},{1,9},{9,17},{17,25},{2,10},{10,18},{18,26},{... | collective-permute-start | bytes 245768 | tf_op jit(solution)/shard_map/ppermute | solution.py:17
  26.8 14.2 %collective-permute-start.1 = (bf16[1,128,320]{1,2,0:T(8,128)(2,1)S(1)}, bf16[1,128,320]{1,2,0:T(8,128)(2,1)S(1)}, u32[]{:S(2)}, u32[]{:S(2)}) collective-permute-start(bf16[1,128,320]{1,2,0:T(8,128)(2,1)S(1)} %get-tuple-element.37), channel_id=1, source_target_pairs={{8,0},{16,8},{24,16},{9,1},{17,9},{25,17},{10,2},{18,10},{26,18},{... | collective-permute-start | bytes 245768 | tf_op jit(solution)/shard_map/ppermute | solution.py:19
  28.2 84.4 %reduce-scatter.4.cloned.1.call-start = ((), (), s32[]{:S(2)}) async-start(), calls=%async_computation.2 | async-start | bytes 4976640
  29.9 26.5 %collective-permute-start.2 = (bf16[1,128,320]{1,2,0:T(8,128)(2,1)}, bf16[1,128,320]{1,2,0:T(8,128)(2,1)}, u32[]{:S(2)}, u32[]{:S(2)}) collective-permute-start(bf16[1,128,320]{1,2,0:T(8,128)(2,1)} %get-tuple-element.32), channel_id=1, source_target_pairs={{0,8},{8,16},{16,24},{1,9},{9,17},{17,25},{2,10},{10,18},{18,26},{... | collective-permute-start | bytes 245768 | tf_op jit(solution)/shard_map/ppermute | solution.py:17
  35.1 21.4 %collective-permute-start.3 = (bf16[1,128,320]{1,2,0:T(8,128)(2,1)}, bf16[1,128,320]{1,2,0:T(8,128)(2,1)}, u32[]{:S(2)}, u32[]{:S(2)}) collective-permute-start(bf16[1,128,320]{1,2,0:T(8,128)(2,1)} %get-tuple-element.33), channel_id=1, source_target_pairs={{8,0},{16,8},{24,16},{9,1},{17,9},{25,17},{10,2},{18,10},{26,18},{... | collective-permute-start | bytes 245768 | tf_op jit(solution)/shard_map/ppermute | solution.py:19
  41.0 0.6 copy-start.17
  44.4 1.4 copy-start.23
  44.4 1.4 copy-start.24
  46.2 0.9 copy-start.18
  47.1 5.4 %copy-start.16 = (bf16[3,128,320]{1,2,0:T(8,128)(2,1)S(1)}, bf16[3,128,320]{1,2,0:T(8,128)(2,1)}, u32[]{:S(2)}) copy-start(bf16[3,128,320]{1,2,0:T(8,128)(2,1)} %get-tuple-element.27) | copy-start | bytes 737284
  47.8 2.0 %copy-start = (f32[9,320,320]{2,1,0:T(8,128)}, f32[9,320,320]{2,1,0:T(8,128)S(1)}, u32[]{:S(2)}) copy-start(f32[9,320,320]{2,1,0:T(8,128)S(1)} %fusion.3) | copy-start | bytes 11059204
  74.1 1.7 %copy-start.9 = (bf16[3,128,320]{2,1,0:T(8,128)(2,1)S(1)}, bf16[3,128,320]{2,1,0:T(8,128)(2,1)}, u32[]{:S(2)}) copy-start(bf16[3,128,320]{2,1,0:T(8,128)(2,1)} %copy.48) | copy-start | bytes 737284
  74.1 2.1 %copy-start.8 = (bf16[3,128,320]{2,1,0:T(8,128)(2,1)S(1)}, bf16[3,128,320]{2,1,0:T(8,128)(2,1)}, u32[]{:S(2)}) copy-start(bf16[3,128,320]{2,1,0:T(8,128)(2,1)} %copy.43) | copy-start | bytes 737284
  74.4 2.2 %copy-start.7 = (bf16[3,128,320]{2,1,0:T(8,128)(2,1)S(1)}, bf16[3,128,320]{2,1,0:T(8,128)(2,1)}, u32[]{:S(2)}) copy-start(bf16[3,128,320]{2,1,0:T(8,128)(2,1)} %copy.44) | copy-start | bytes 737284
  75.8 1.1 copy-start.6
  76.6 1.1 copy-start.20
  77.6 1.0 copy-start.5
  81.9 3.0 %copy-start.14 = (bf16[3,128,320]{2,1,0:T(8,128)(2,1)S(1)}, bf16[3,128,320]{2,1,0:T(8,128)(2,1)}, u32[]{:S(2)}) copy-start(bf16[3,128,320]{2,1,0:T(8,128)(2,1)} %copy.56) | copy-start | bytes 737284
  81.9 3.4 %copy-start.13 = (bf16[3,128,320]{2,1,0:T(8,128)(2,1)S(1)}, bf16[3,128,320]{2,1,0:T(8,128)(2,1)}, u32[]{:S(2)}) copy-start(bf16[3,128,320]{2,1,0:T(8,128)(2,1)} %copy.57) | copy-start | bytes 737284
  85.0 1.0 copy-start.4
  85.4 1.0 copy-start.12
  85.9 1.0 copy-start.10
  86.3 1.0 copy-start.11
  86.9 1.1 copy-start.21
  86.9 1.1 copy-start.22
  89.4 13.4 %copy-start.3 = (f32[1,3,128,320]{2,3,1,0:T(8,128)S(1)}, f32[1,3,128,320]{2,3,1,0:T(8,128)}, u32[]{:S(2)}) copy-start(f32[1,3,128,320]{2,3,1,0:T(8,128)} %copy.53) | copy-start | bytes 1474564
  113.9 23.4 %copy-start.2 = (f32[360,320]{1,0:T(8,128)S(1)}, f32[360,320]{1,0:T(8,128)}, u32[]{:S(2)}) copy-start(f32[360,320]{1,0:T(8,128)} %copy.69) | copy-start | bytes 1382404
Sparse Core Ops, SparseCore 0:
  28.3 27.9 all-gather.4
  59.8 52.7 reduce-scatter.3
